TPU v7x, 256 devices: a whole 4x4x8 slice. The times are simulated.
256 devices in a mesh: gx: 8 (over x, core), gy: 32 (over y, z).
Axes of the slice: x: 4, y: 4, z: 8, core: 2. Of those that a mesh axis runs over, the one named last changes fastest.
Arguments:
- hidden_in: bfloat16 [8192, 4096], P('gx', 'gy')
- norm_gain: bfloat16 [4096], P('gy'), may hold values from 0.099609375 to 1.8984375
- query_proj: bfloat16 [4096, 4096], P('gx', 'gy')
- kv_proj: bfloat16 [1024, 4096], P(None, 'gy')
- prompt_lengths: int32 [8], replicated, may hold values from 1 to 4096, 8192 in all
- cache_slot: int32 [512], replicated, may hold values from 0 to 511, as said below
Outputs:
- attention: bfloat16 [8192, 4096], P('gy', 'gx')
- kv_cache: bfloat16 [512, 16, 1024], P('gy', None, 'gx')
Inputs may be any that keep to these rules, and one draw needn't show every extreme that they name: `prompt_lengths`: the 8 prompts sum to 8192 tokens; the longest has exactly 4096. `cache_slot`: A permutation of the 512 slots; slot s is held by index s // 16 of gy. The 16 pages of one token block go to any one index at most 1 times, and every index receives exactly 16 pages.
All inputs are finite; a program needn't handle non-finite values.
Results may differ from a plain program's by a relative error of at most 0.0066.
The roundings to bfloat16 on the way count: a program that leaves them out, or rounds other values in their place, can miss the bound.
Values may be sent and summed in bfloat16 or wider, within the bound.
No kernel may reach another device: no remote copies, remote signals or barrier semaphores. Data moves between devices by JAX's collectives and lax.ppermute only.
A program may use at most 128 MiB of HBM per device.

v0:
```python
import math
import jax
import jax.numpy as jnp
from jax import lax
from jax.sharding import PartitionSpec as P

D = 4096
H = 32
KVH = 4
HD = 128
PAGES_DEV = 16
epsilon = 1e-06
rope_base = 5000000.0
masked_out = -1e30


def token_places(prompt_lengths, token_index):
    prompt_ends = jnp.cumsum(prompt_lengths)
    prompt_starts = prompt_ends - prompt_lengths
    segment = jnp.sum((token_index[:, None] >= prompt_ends[None, :]).astype(jnp.int32), axis=1)
    chosen = segment[:, None] == jnp.arange(prompt_lengths.shape[0], dtype=jnp.int32)[None, :]
    opening = jnp.sum(jnp.where(chosen, prompt_starts[None, :], 0), axis=1)
    return (segment, token_index - opening)


def rotate(vectors, places):
    half_size = vectors.shape[-1] // 2
    frequency = rope_base ** (-(jnp.arange(half_size, dtype=jnp.float32) * 2.0) / vectors.shape[-1])
    angles = places.astype(jnp.float32)[:, None] * frequency[None, :]
    cos_part = jnp.cos(angles)[:, None, :]
    sin_part = jnp.sin(angles)[:, None, :]
    leading = vectors[..., :half_size]
    trailing = vectors[..., half_size:]
    return jnp.concatenate(
        [leading * cos_part - trailing * sin_part, trailing * cos_part + leading * sin_part],
        axis=-1,
    )


def local(hidden_in, norm_gain, query_proj, kv_proj, prompt_lengths, cache_slot):
    count_gx = lax.axis_size("gx")
    count_gy = lax.axis_size("gy")
    where_gx = lax.axis_index("gx")
    where_gy = lax.axis_index("gy")
    local_rows = hidden_in.shape[0]
    block_tokens = local_rows * count_gx // count_gy
    all_tokens = block_tokens * count_gy
    heads_here = query_proj.shape[0] // HD
    group_size = H // KVH
    kv_head = where_gx * heads_here // group_size
    contract = (((1,), (1,)), ((), ()))
    kv_width = 2 * HD
    kv_start = kv_head * 2 * HD
    kv_rows = lax.dynamic_slice_in_dim(kv_proj, kv_start, kv_width, 0)
    widened = hidden_in.astype(jnp.float32)
    squares = jnp.sum(widened * widened, axis=1)
    totals = lax.psum(squares, "gy")
    normed = (
        widened * lax.rsqrt(totals / D + epsilon)[:, None] * norm_gain.astype(jnp.float32)[None, :]
    ).astype(jnp.bfloat16)
    gathered = lax.all_gather(normed, "gx", axis=0, tiled=True)
    stacked = jnp.concatenate([query_proj, kv_rows], axis=0)
    projected = lax.psum_scatter(
        lax.dot_general(gathered, stacked, contract, preferred_element_type=jnp.float32),
        "gy",
        scatter_dimension=0,
        tiled=True,
    )
    every_index = jnp.arange(all_tokens, dtype=jnp.int32)
    segment_all, place_all = token_places(prompt_lengths, every_index)
    first_query = where_gy * block_tokens
    token_index = first_query + jnp.arange(block_tokens, dtype=jnp.int32)
    segment_own = lax.dynamic_slice_in_dim(segment_all, first_query, block_tokens, 0)
    place_own = lax.dynamic_slice_in_dim(place_all, first_query, block_tokens, 0)
    query_cols = heads_here * HD
    queries = rotate(
        projected[:, :query_cols].reshape(block_tokens, heads_here, HD), place_own
    ).astype(jnp.bfloat16)
    keys = rotate(projected[:, query_cols : query_cols + HD][:, None, :], place_own)[
        :, 0, :
    ].astype(jnp.bfloat16)
    values = projected[:, query_cols + HD :].astype(jnp.bfloat16)
    cache_cols = jnp.where(where_gx % 2 == 0, keys, values)
    score_scale = 1.0 / math.sqrt(HD)
    last_query = first_query + block_tokens - 1
    first_segment = segment_own[0]
    initial = (
        jnp.full((heads_here, block_tokens), masked_out, jnp.float32),
        jnp.zeros((heads_here, block_tokens), jnp.float32),
        jnp.zeros((heads_here, block_tokens, HD), jnp.float32),
    )
    key_piece = lax.all_gather(keys, "gy", axis=0, tiled=True)
    value_piece = lax.all_gather(values, "gy", axis=0, tiled=True)
    block_count = key_piece.shape[0] // block_tokens
    key_blocks = key_piece.reshape(block_count, block_tokens, HD)
    value_blocks = value_piece.reshape(block_count, block_tokens, HD)

    def one_block(current, inputs):
        key_rows, value_rows, offset = inputs
        block_begin = offset * block_tokens
        key_segment = lax.dynamic_slice_in_dim(segment_all, block_begin, block_tokens, 0)
        skipped = jnp.logical_or(
            block_begin > last_query, key_segment[block_tokens - 1] < first_segment
        )

        def compute(previous):
            running_max, running_sum, running_acc = previous
            key_index = block_begin + jnp.arange(block_tokens, dtype=jnp.int32)
            allowed = (key_segment[None, :] == segment_own[:, None]) & (
                key_index[None, :] <= token_index[:, None]
            )
            scores = (
                jnp.einsum("qhd,kd->hqk", queries, key_rows, preferred_element_type=jnp.float32)
                * score_scale
            )
            scores = jnp.where(allowed[None], scores, masked_out)
            new_max = jnp.maximum(running_max, jnp.max(scores, axis=2))
            weights = jnp.where(allowed[None], jnp.exp(scores - new_max[..., None]), 0.0)
            factor = jnp.exp(running_max - new_max)
            new_sum = running_sum * factor + jnp.sum(weights, axis=2)
            update = jnp.einsum(
                "hqk,kd->hqd",
                weights.astype(jnp.bfloat16),
                value_rows,
                preferred_element_type=jnp.float32,
            )
            return (new_max, new_sum, running_acc * factor[..., None] + update)

        return (lax.cond(skipped, lambda previous: previous, compute, current), None)

    offsets = jnp.arange(block_count, dtype=jnp.int32)
    result, unused = lax.scan(one_block, initial, (key_blocks, value_blocks, offsets))
    final_max, final_sum, final_acc = result
    attention = (
        (final_acc / final_sum[..., None])
        .transpose(1, 0, 2)
        .reshape(block_tokens, query_cols)
        .astype(jnp.bfloat16)
    )
    pages_dev = PAGES_DEV
    page_len = block_tokens // pages_dev
    width_cols = cache_cols.shape[1]
    my_pages = cache_cols.reshape(pages_dev, page_len * width_cols)
    capacity = max(1, pages_dev // count_gy)
    slots_all = count_gy * capacity
    owners = (cache_slot // pages_dev).reshape(count_gy, pages_dev)
    page_range = jnp.arange(pages_dev, dtype=jnp.int32)
    earlier = page_range[None, :] < page_range[:, None]
    same_owner = owners[:, :, None] == owners[:, None, :]
    ranks = jnp.sum((same_owner & earlier[None]).astype(jnp.int32), axis=2)
    my_owner = lax.dynamic_index_in_dim(owners, where_gy, 0, keepdims=False)
    my_rank = lax.dynamic_index_in_dim(ranks, where_gy, 0, keepdims=False)
    target = my_owner * capacity + my_rank
    slot_range = jnp.arange(slots_all, dtype=jnp.int32)
    send_map = (slot_range[:, None] == target[None, :]).astype(jnp.bfloat16)
    outgoing = jnp.dot(send_map, my_pages, preferred_element_type=jnp.float32).astype(jnp.bfloat16)
    incoming = lax.all_to_all(outgoing, "gy", split_axis=0, concat_axis=0, tiled=True)
    wanted = where_gy * pages_dev + page_range
    matches = cache_slot[None, :] == wanted[:, None]
    page_ids = jnp.arange(cache_slot.shape[0], dtype=jnp.int32)
    source_page = jnp.sum(jnp.where(matches, page_ids[None, :], 0), axis=1)
    source_rank = jnp.sum(jnp.where(matches, ranks.reshape(-1)[None, :], 0), axis=1)
    source_slot = source_page // pages_dev * capacity + source_rank
    take_map = (source_slot[:, None] == slot_range[None, :]).astype(jnp.bfloat16)
    cache_block = jnp.dot(take_map, incoming, preferred_element_type=jnp.float32)
    cache_block = cache_block.astype(jnp.bfloat16).reshape(pages_dev, page_len, width_cols)
    return (attention, cache_block)


def solution(mesh):
    return jax.shard_map(
        local,
        mesh=mesh,
        in_specs=(P("gx", "gy"), P("gy"), P("gx", "gy"), P(None, "gy"), P(), P()),
        out_specs=(P("gy", "gx"), P("gy", None, "gx")),
        check_vma=False,
    )
```

profile of v0, /device:TPU:208, one launch (start us, length us, event | category | flops | bytes accessed | tf_op | source)
XLA Modules:
  0.0 692.0 jit_solution(10577667807313542377)
XLA Ops:
  7.2 1.2 fusion.19
  8.4 58.9 %psum.7 = f32[1024]{0:T(1024)S(1)} all-reduce(f32[1024]{0:T(1024)S(1)} %fusion.19), channel_id=1, replica_groups=mesh['gx'=8,'gy'=32] {'gy'}, use_global_device_ids=true, to_apply=%region_1.2 | all-reduce | flops 1024 | bytes 8192 | tf_op jit(solution)/shard_map/psum | solution.py:57
  67.3 0.7 convert_element_type.52
  67.9 1.9 fusion.21
  69.9 38.3 %all-gather.5.cloned.1.call-done = bf16[8192,128]{1,0:T(8,128)(2,1)} async-done(((bf16[1024,128]{1,0:T(8,128)(2,1)}), bf16[8192,128]{1,0:T(8,128)(2,1)}) %all-gather.5.cloned.1.call-update) | async-done | bytes 2097168 | tf_op jit(solution)/shard_map/all_gather | solution.py:61
  108.2 13.3 %fusion.23 = f32[8192,768]{0,1:T(8,128)} fusion(bf16[8192,128]{1,0:T(8,128)(2,1)} %all-gather.5.cloned.1.call-done, bf16[256,128]{1,0:T(8,128)(2,1)S(1)} %constant_dynamic-slice_fusion, bf16[512,128]{1,0:T(8,128)(2,1)} %param.12), kind=kOutput, calls=%fused_computation.42 | convolution fusion | flops 1611005952 | bytes 27459584 | tf_op jit(solution)/shard_map/dot_general | solution.py:64
  122.8 264.6 %reduce-scatter.2.cloned.1.call-done = f32[256,768]{0,1:T(8,128)} async-done(((f32[8192,768]{0,1:T(8,128)}), f32[256,768]{0,1:T(8,128)}) %reduce-scatter.2.cloned.1.call-update) | async-done | bytes 786448 | tf_op jit(solution)/shard_map/reduce_scatter | solution.py:63
  387.5 1.0 slice_bitcast_fusion
  388.8 1.5 bitcast_select_fusion
  390.4 0.6 pad_maximum_fusion.1
  394.4 0.7 reduce.2
  395.0 0.7 reshape.266
  395.8 10.1 %all-to-all-start = ((bf16[32,2,1024]{2,1,0:T(2,128)(2,1)}), bf16[32,2,1024]{2,1,0:T(2,128)(2,1)S(1)}, u32[]{:S(2)}, u32[]{:S(2)}) async-start(bf16[32,2,1024]{2,1,0:T(2,128)(2,1)} %reshape.266), calls=%async_computation.1 | async-start | bytes 262144 | tf_op jit(solution)/shard_map/all_to_all | solution.py:157
  406.2 5.9 all-to-all-done
  412.4 0.6 copy.77
  413.1 52.7 %all-gather.7.cloned.1.call-done = bf16[8192,128]{0,1:T(8,128)(2,1)} async-done(((bf16[256,128]{0,1:T(8,128)(2,1)}), bf16[8192,128]{0,1:T(8,128)(2,1)}) %all-gather.7.cloned.1.call-update) | async-done | bytes 2097168 | tf_op jit(solution)/shard_map/all_gather | solution.py:93
  465.7 3.2 copy.72
  469.0 72.9 %all-gather.9.cloned.1.call-done = bf16[8192,1,128]{0,2,1:T(8,128)(2,1)} async-done(((bf16[256,1,128]{0,2,1:T(8,128)(2,1)}), bf16[8192,1,128]{0,2,1:T(8,128)(2,1)}) %all-gather.9.cloned.1.call-update) | async-done | bytes 2097168 | tf_op jit(solution)/shard_map/all_gather | solution.py:92
  541.8 4.1 copy.71
  546.0 138.6 %while.15 = (s32[]{:T(128)}, f32[4,256]{1,0:T(4,128)S(1)}, f32[4,256]{1,0:T(4,128)S(1)}, f32[4,256,128]{2,1,0:T(8,128)S(1)}, s32[32]{0:T(128)S(1)}, /*index=5*/s...) while((s32[]{:T(128)}, f32[4,256]{1,0:T(4,128)S(1)}, ...), condition=%wide.region_11.12_spmd.clone, body=%wide.region_6.11_spmd.clone.sunk | while | flops 137038352 | bytes 4926361 | solution.py:132
  547.3 0.6 slice.55
  550.6 0.6 slice.55
  553.8 0.6 slice.55
  557.0 0.6 slice.55
  560.3 0.6 slice.55
  563.5 0.6 slice.55
  566.7 0.6 slice.55
  568.6 2.1 conditional.3
  568.7 1.2 fusion.46
  572.0 0.6 slice.55
  573.9 2.1 conditional.3
  574.0 1.2 fusion.46
  577.3 0.6 slice.55
  579.2 2.1 conditional.3
  579.3 1.2 fusion.46
  584.5 2.1 conditional.3
  584.6 1.2 fusion.46
  589.8 2.1 conditional.3
  589.9 1.2 fusion.46
  595.1 2.1 conditional.3
  595.2 1.2 fusion.46
  600.4 2.1 conditional.3
  600.5 1.2 fusion.46
  605.7 2.1 conditional.3
  605.8 1.2 fusion.46
  611.0 2.1 conditional.3
  611.1 1.2 fusion.46
  616.3 2.1 conditional.3
  616.4 1.2 fusion.46
  621.6 2.1 conditional.3
  621.7 1.2 fusion.46
  626.9 2.1 conditional.3
  627.0 1.2 fusion.46
  632.2 2.1 conditional.3
  632.3 1.2 fusion.46
  637.5 2.1 conditional.3
  637.6 1.2 fusion.46
  642.8 2.1 conditional.3
  642.9 1.2 fusion.46
  648.1 2.1 conditional.3
  648.2 1.2 fusion.46
  653.4 2.1 conditional.3
  653.5 1.2 fusion.46
  684.6 0.9 copy_bitcast_fusion
  (337 shorter events, 56.0 us)
Async XLA Ops:
  7.2 62.7 %copy-start = (bf16[1024,128]{1,0:T(8,128)(2,1)S(1)}, bf16[1024,128]{1,0:T(8,128)(2,1)}, u32[]{:S(2)}) copy-start(bf16[1024,128]{1,0:T(8,128)(2,1)} %param.13) | copy-start | bytes 786436
  7.2 101.1 %all-gather.5.cloned.1.call-start = ((), (), s32[]{:S(2)}) async-start(), calls=%async_computation.2 | async-start | bytes 2359296 | tf_op jit(solution)/shard_map/all_gather | solution.py:61
  69.8 317.6 %reduce-scatter.2.cloned.1.call-start = ((), (), s32[]{:S(2)}) async-start(), calls=%async_computation.3 | async-start | bytes 25952256 | tf_op jit(solution)/shard_map/reduce_scatter | solution.py:63
  121.6 0.7 copy-start.2
  121.6 270.1 %copy-start.1 = (s32[512]{0:T(512)S(1)}, s32[512]{0:T(512)}, u32[]{:S(2)}) copy-start(s32[512]{0:T(512)} %param.15) | copy-start | bytes 6148
  121.6 344.1 %all-gather.7.cloned.1.call-start = ((), (), s32[]{:S(2)}) async-start(), calls=%async_computation.4 | async-start | bytes 2162688 | tf_op jit(solution)/shard_map/all_gather | solution.py:93
  387.5 5.6 slice-start
  390.3 151.5 %all-gather.9.cloned.1.call-start = ((), (), s32[]{:S(2)}) async-start(), calls=%async_computation.5 | async-start | bytes 2162688 | tf_op jit(solution)/shard_map/all_gather | solution.py:92
  395.8 16.3 %all-to-all-start = ((bf16[32,2,1024]{2,1,0:T(2,128)(2,1)}), bf16[32,2,1024]{2,1,0:T(2,128)(2,1)S(1)}, u32[]{:S(2)}, u32[]{:S(2)}) async-start(bf16[32,2,1024]{2,1,0:T(2,128)(2,1)} %reshape.266), calls=%async_computation.1 | async-start | bytes 262144 | tf_op jit(solution)/shard_map/all_to_all | solution.py:157
Sparse Core Ops, SparseCore 0:
  69.9 38.2 all-gather.4
  121.7 265.7 reduce-scatter.1
  390.5 75.2 all-gather.6
  468.1 73.7 all-gather.8
where the time goes:
time: 694 us; the launch traced here: 692 us
  waiting for transfers between devices  434 us (63%)
  loops' own time  63.5 us (9%)
  blocking collectives  58.9 us (8%)
  local copies, waits for them, and re-layouts  52.8 us (8%)
  matrix products  42.2 us (6%)
  other arithmetic  16 us (2%)
  between operations  14 us (2%)
  starting transfers between devices  10.3 us (1%)
    reduce_scatter x1, waiting for transfers between devices, local(): lax.psum_scatter(lax.dot_general(gathered, stacked, contract, preferred_e...  265 us
    all_gather x1, waiting for transfers between devices, local(): key_piece = lax.all_gather(keys, 'gy', axis=0, tiled=True)  72.9 us
    another operation x1, loops' own time, local(): lax.scan(one_block, initial, (key_blocks, value_blocks, offsets))  62.1 us
    psum x1, blocking collectives, local(): totals = lax.psum(squares, 'gy')  58.9 us
    all_gather x1, waiting for transfers between devices, local(): value_piece = lax.all_gather(values, 'gy', axis=0, tiled=True)  52.7 us
    all_gather x1, waiting for transfers between devices, local(): gathered = lax.all_gather(normed, 'gx', axis=0, tiled=True)  38.3 us
    dot_general x17, matrix products, compute(): jnp.einsum('qhd,kd->hqk', queries, key_rows, preferred_element_type=jnp.f...  19.9 us
    slice x32, local copies, waits for them, and re-layouts, one_block(): key_segment[block_tokens - 1] < first_segment  18.9 us
  transfers between devices with their start and end apart: 5, of which 5 were waited for; matrix products, arithmetic and copies ran while one was open for 1% of the time, Pallas kernels for 0%

commit v1 on v0

--- a/solution.py
+++ b/solution.py
@@ -54,7 +54,7 @@
     kv_rows = lax.dynamic_slice_in_dim(kv_proj, kv_start, kv_width, 0)
     widened = hidden_in.astype(jnp.float32)
     squares = jnp.sum(widened * widened, axis=1)
-    totals = lax.psum(squares, "gy")
+    totals = jnp.sum(lax.all_gather(squares, "gy"), axis=0)
     normed = (
         widened * lax.rsqrt(totals / D + epsilon)[:, None] * norm_gain.astype(jnp.float32)[None, :]
     ).astype(jnp.bfloat16)

time: 694 us -> 667 us (0.961)
  blocking collectives: 58.9 us -> 40.1 us
  waiting for transfers between devices: 434 us -> 426 us
    psum x1 -> x0, blocking collectives: 58.9 us -> none  [local(): totals = lax.psum(squares, 'gy')]
    all_gather x0 -> x1, blocking collectives: none -> 40.1 us  [local(): totals = jnp.sum(lax.all_gather(squares, 'gy'), axis=0)]
    all_gather x1, waiting for transfers between devices: 38.3 us -> 29.7 us  [local(): gathered = lax.all_gather(normed, 'gx', axis=0, tiled=True)]
  transfers between devices with their start and end apart: 5 -> 5, of which waited for: 5 -> 5; matrix products, arithmetic and copies ran while one was open for 1% -> 2% of each run, Pallas kernels for 0% -> 0%
where the time goes in v1:
time: 667 us; the launch traced here: 665 us
  waiting for transfers between devices  426 us (64%)
  loops' own time  63.5 us (10%)
  local copies, waits for them, and re-layouts  52.8 us (8%)
  matrix products  42.2 us (6%)
  blocking collectives  40.1 us (6%)
  other arithmetic  16 us (2%)
  between operations  14 us (2%)
  starting transfers between devices  10.3 us (2%)
    reduce_scatter x1, waiting for transfers between devices, local(): lax.psum_scatter(lax.dot_general(gathered, stacked, contract, preferred_e...  264 us
    all_gather x1, waiting for transfers between devices, local(): key_piece = lax.all_gather(keys, 'gy', axis=0, tiled=True)  72.9 us
    another operation x1, loops' own time, local(): lax.scan(one_block, initial, (key_blocks, value_blocks, offsets))  62.1 us
    all_gather x1, waiting for transfers between devices, local(): value_piece = lax.all_gather(values, 'gy', axis=0, tiled=True)  52.7 us
    all_gather x1, blocking collectives, local(): totals = jnp.sum(lax.all_gather(squares, 'gy'), axis=0)  40.1 us
    all_gather x1, waiting for transfers between devices, local(): gathered = lax.all_gather(normed, 'gx', axis=0, tiled=True)  29.7 us
    dot_general x17, matrix products, compute(): jnp.einsum('qhd,kd->hqk', queries, key_rows, preferred_element_type=jnp.f...  19.9 us
    slice x32, local copies, waits for them, and re-layouts, one_block(): key_segment[block_tokens - 1] < first_segment  18.9 us
  transfers between devices with their start and end apart: 5, of which 5 were waited for; matrix products, arithmetic and copies ran while one was open for 2% of the time, Pallas kernels for 0%

profile of v1, /device:TPU:208, one launch (start us, length us, event | category | flops | bytes accessed | tf_op | source)
XLA Modules:
  0.0 664.6 jit_solution(13416813856976006922)
XLA Ops:
  7.2 1.2 fusion.19
  8.4 40.1 %all-gather = f32[32768]{0:T(1024)S(1)} all-gather(f32[1024]{0:T(1024)S(1)} %fusion.19), channel_id=2, replica_groups=mesh['gx'=8,'gy'=32] {'gy'}, dimensions={0}, use_global_device_ids=true | all-gather | bytes 135168 | tf_op jit(solution)/shard_map/all_gather | solution.py:57
  48.6 0.7 convert_element_type.52
  49.3 1.9 fusion.21
  51.2 29.7 %all-gather.6.cloned.1.call-done = bf16[8192,128]{1,0:T(8,128)(2,1)} async-done(((bf16[1024,128]{1,0:T(8,128)(2,1)}), bf16[8192,128]{1,0:T(8,128)(2,1)}) %all-gather.6.cloned.1.call-update) | async-done | bytes 2097168 | tf_op jit(solution)/shard_map/all_gather | solution.py:61
  80.9 13.3 %fusion.23 = f32[8192,768]{0,1:T(8,128)} fusion(bf16[8192,128]{1,0:T(8,128)(2,1)} %all-gather.6.cloned.1.call-done, bf16[256,128]{1,0:T(8,128)(2,1)S(1)} %constant_dynamic-slice_fusion, bf16[512,128]{1,0:T(8,128)(2,1)} %param.12), kind=kOutput, calls=%fused_computation.42 | convolution fusion | flops 1611005952 | bytes 27459584 | tf_op jit(solution)/shard_map/dot_general | solution.py:64
  95.5 264.4 %reduce-scatter.2.cloned.1.call-done = f32[256,768]{0,1:T(8,128)} async-done(((f32[8192,768]{0,1:T(8,128)}), f32[256,768]{0,1:T(8,128)}) %reduce-scatter.2.cloned.1.call-update) | async-done | bytes 786448 | tf_op jit(solution)/shard_map/reduce_scatter | solution.py:63
  360.0 1.0 slice_bitcast_fusion
  361.3 1.5 bitcast_select_fusion
  362.9 0.6 pad_maximum_fusion.1
  366.9 0.7 reduce.2
  367.5 0.7 reshape.271
  368.3 10.1 %all-to-all-start = ((bf16[32,2,1024]{2,1,0:T(2,128)(2,1)}), bf16[32,2,1024]{2,1,0:T(2,128)(2,1)S(1)}, u32[]{:S(2)}, u32[]{:S(2)}) async-start(bf16[32,2,1024]{2,1,0:T(2,128)(2,1)} %reshape.271), calls=%async_computation.1 | async-start | bytes 262144 | tf_op jit(solution)/shard_map/all_to_all | solution.py:157
  378.7 5.9 all-to-all-done
  384.9 0.6 copy.77
  385.6 52.7 %all-gather.8.cloned.1.call-done = bf16[8192,128]{0,1:T(8,128)(2,1)} async-done(((bf16[256,128]{0,1:T(8,128)(2,1)}), bf16[8192,128]{0,1:T(8,128)(2,1)}) %all-gather.8.cloned.1.call-update) | async-done | bytes 2097168 | tf_op jit(solution)/shard_map/all_gather | solution.py:93
  438.3 3.2 copy.72
  441.5 72.9 %all-gather.10.cloned.1.call-done = bf16[8192,1,128]{0,2,1:T(8,128)(2,1)} async-done(((bf16[256,1,128]{0,2,1:T(8,128)(2,1)}), bf16[8192,1,128]{0,2,1:T(8,128)(2,1)}) %all-gather.10.cloned.1.call-update) | async-done | bytes 2097168 | tf_op jit(solution)/shard_map/all_gather | solution.py:92
  514.4 4.1 copy.71
  518.5 138.6 %while.15 = (s32[]{:T(128)}, f32[4,256]{1,0:T(4,128)S(1)}, f32[4,256]{1,0:T(4,128)S(1)}, f32[4,256,128]{2,1,0:T(8,128)S(1)}, s32[32]{0:T(128)S(1)}, /*index=5*/s...) while((s32[]{:T(128)}, f32[4,256]{1,0:T(4,128)S(1)}, ...), condition=%wide.region_11.12_spmd.clone, body=%wide.region_6.11_spmd.clone.sunk | while | flops 137038352 | bytes 4926361 | solution.py:132
  519.9 0.6 slice.55
  523.1 0.6 slice.55
  526.3 0.6 slice.55
  529.5 0.6 slice.55
  532.8 0.6 slice.55
  536.0 0.6 slice.55
  539.2 0.6 slice.55
  541.1 2.1 conditional.3
  541.2 1.2 fusion.46
  544.5 0.6 slice.55
  546.4 2.1 conditional.3
  546.6 1.2 fusion.46
  549.8 0.6 slice.55
  551.7 2.1 conditional.3
  551.9 1.2 fusion.46
  557.0 2.1 conditional.3
  557.2 1.2 fusion.46
  562.3 2.1 conditional.3
  562.5 1.2 fusion.46
  567.6 2.1 conditional.3
  567.8 1.2 fusion.46
  572.9 2.1 conditional.3
  573.1 1.2 fusion.46
  578.2 2.1 conditional.3
  578.4 1.2 fusion.46
  583.5 2.1 conditional.3
  583.7 1.2 fusion.46
  588.8 2.1 conditional.3
  589.0 1.2 fusion.46
  594.1 2.1 conditional.3
  594.3 1.2 fusion.46
  599.4 2.1 conditional.3
  599.6 1.2 fusion.46
  604.7 2.1 conditional.3
  604.9 1.2 fusion.46
  610.0 2.1 conditional.3
  610.2 1.2 fusion.46
  615.3 2.1 conditional.3
  615.5 1.2 fusion.46
  620.6 2.1 conditional.3
  620.8 1.2 fusion.46
  625.9 2.1 conditional.3
  626.1 1.2 fusion.46
  657.1 0.9 copy_bitcast_fusion
  (339 shorter events, 56.0 us)
Async XLA Ops:
  7.2 44.1 %copy-start = (bf16[1024,128]{1,0:T(8,128)(2,1)S(1)}, bf16[1024,128]{1,0:T(8,128)(2,1)}, u32[]{:S(2)}) copy-start(bf16[1024,128]{1,0:T(8,128)(2,1)} %param.13) | copy-start | bytes 786436
  7.2 73.7 %all-gather.6.cloned.1.call-start = ((), (), s32[]{:S(2)}) async-start(), calls=%async_computation.2 | async-start | bytes 2359296 | tf_op jit(solution)/shard_map/all_gather | solution.py:61
  51.1 308.8 %reduce-scatter.2.cloned.1.call-start = ((), (), s32[]{:S(2)}) async-start(), calls=%async_computation.3 | async-start | bytes 25952256 | tf_op jit(solution)/shard_map/reduce_scatter | solution.py:63
  94.3 0.7 copy-start.2
  94.3 269.9 %copy-start.1 = (s32[512]{0:T(512)S(1)}, s32[512]{0:T(512)}, u32[]{:S(2)}) copy-start(s32[512]{0:T(512)} %param.15) | copy-start | bytes 6148
  94.3 344.0 %all-gather.8.cloned.1.call-start = ((), (), s32[]{:S(2)}) async-start(), calls=%async_computation.4 | async-start | bytes 2162688 | tf_op jit(solution)/shard_map/all_gather | solution.py:93
  360.0 5.6 slice-start
  362.8 151.5 %all-gather.10.cloned.1.call-start = ((), (), s32[]{:S(2)}) async-start(), calls=%async_computation.5 | async-start | bytes 2162688 | tf_op jit(solution)/shard_map/all_gather | solution.py:92
  368.3 16.3 %all-to-all-start = ((bf16[32,2,1024]{2,1,0:T(2,128)(2,1)}), bf16[32,2,1024]{2,1,0:T(2,128)(2,1)S(1)}, u32[]{:S(2)}, u32[]{:S(2)}) async-start(bf16[32,2,1024]{2,1,0:T(2,128)(2,1)} %reshape.271), calls=%async_computation.1 | async-start | bytes 262144 | tf_op jit(solution)/shard_map/all_to_all | solution.py:157
Sparse Core Ops, SparseCore 0:
  51.3 29.6 all-gather.5
  94.4 265.5 reduce-scatter.1
  362.9 75.2 all-gather.7
  440.6 73.7 all-gather.9
